TPU v7x, 512 devices: a whole 4x8x8 slice. The times are simulated.
512 devices in a mesh: gx: 32 (over x, z), gy: 16 (over y, core).
Axes of the slice: x: 4, y: 8, z: 8, core: 2. Of those that a mesh axis runs over, the one named last changes fastest.
Arguments:
- start_disp: float32 [6, 3, 128, 128, 128], P(None, None, 'gx', 'gy'), may hold values from -6 to 6
- bone_mask: int32 [128, 128, 128], P('gx', 'gy'), may hold values from 0 to 1, as said below
- density: float32 [128, 128, 128], P('gx', 'gy'), may hold values from 0.3 to 1
- load_nodes: int32 [32, 16, 6, 32], P('gx', 'gy'), may hold values from 0 to 31
- load_forces: float32 [32, 16, 6, 3, 32], P('gx', 'gy'), may hold values from -12 to 12
Outputs:
- displacement: float32 [6, 3, 128, 128, 128], P(None, None, 'gx', 'gy')
- new_density: float32 [128, 128, 128], P('gx', 'gy')
Inputs may be any that keep to these rules, and one draw needn't show every extreme that they name: `bone_mask`: 1 marks a bone voxel.
All inputs are finite; a program needn't handle non-finite values.
Results may differ from a plain program's by a relative error of at most 0.0001.
Values sent between devices are 32-bit elements; how exact they have to be, the bound alone decides.
No kernel may reach another device: no remote copies, remote signals or barrier semaphores. Data moves between devices by JAX's collectives and lax.ppermute only.
A program may use at most 64 MiB of HBM per device.

v0:
```python
import jax
import jax.numpy as jnp
import numpy as np
from jax import lax
from jax.sharding import PartitionSpec as P

spring = 0.1
poisson = 0.3
blur_sigma = 2.0
density_cap = 1.0
mean_eps = 1e-06
highest = lax.Precision.HIGHEST


def from_behind(block, axis, distance):
    devices = range(lax.axis_size(axis))
    route = [(i - distance, i) for i in devices if i - distance in devices]
    return lax.ppermute(block, axis, route)


def with_halo(cells, sides, width):
    for axis, dim in sides:
        count = lax.axis_size(axis)
        ends = count - 1
        head = lax.slice_in_dim(cells, 0, width, axis=dim)
        tail = lax.slice_in_dim(cells, cells.shape[dim] - width, cells.shape[dim], axis=dim)
        cells = jnp.concatenate(
            [
                lax.ppermute(tail, axis, [(i, (i + 1) % count) for i in range(ends)]),
                cells,
                lax.ppermute(head, axis, [((i + 1) % count, i) for i in range(ends)]),
            ],
            axis=dim,
        )
    return cells


def hex_stiffness():
    lame_first = poisson / ((1.0 + poisson) * (1.0 - 2.0 * poisson))
    shear_mod = 1.0 / (2.0 * (1.0 + poisson))
    elastic = np.zeros((6, 6))
    elastic[:3, :3] = lame_first
    for axis_id in range(3):
        elastic[axis_id, axis_id] = lame_first + 2.0 * shear_mod
        elastic[axis_id + 3, axis_id + 3] = shear_mod
    points = [0.5 - 0.5 / np.sqrt(3.0), 0.5 + 0.5 / np.sqrt(3.0)]
    stiffness = np.zeros((24, 24))
    for point_x in points:
        for point_y in points:
            for point_z in points:
                coords = (point_x, point_y, point_z)
                strain = np.zeros((6, 24))
                for corner in range(8):
                    offsets = (corner // 4, corner // 2 % 2, corner % 2)
                    shapes = [
                        coords[axis_id] if offsets[axis_id] == 1 else 1.0 - coords[axis_id]
                        for axis_id in range(3)
                    ]
                    slopes = [1.0 if offsets[axis_id] == 1 else -1.0 for axis_id in range(3)]
                    grad_x = slopes[0] * shapes[1] * shapes[2]
                    grad_y = shapes[0] * slopes[1] * shapes[2]
                    grad_z = shapes[0] * shapes[1] * slopes[2]
                    column = 3 * corner
                    strain[0, column] = grad_x
                    strain[1, column + 1] = grad_y
                    strain[2, column + 2] = grad_z
                    strain[3, column] = grad_y
                    strain[3, column + 1] = grad_x
                    strain[4, column + 1] = grad_z
                    strain[4, column + 2] = grad_y
                    strain[5, column] = grad_z
                    strain[5, column + 2] = grad_x
                stiffness += 0.125 * strain.T @ elastic @ strain
    return stiffness


def blur_weights():
    offsets = np.arange(9) - 4.0
    unscaled = np.exp(-offsets * offsets / (2.0 * blur_sigma * blur_sigma))
    return [float(entry) for entry in unscaled / unscaled.sum()]


def blur_valid(values, axis_id, extent):
    weights = blur_weights()
    summed = weights[0] * lax.slice_in_dim(values, 0, extent, axis=axis_id)
    for tap_index in range(1, 9):
        summed = summed + weights[tap_index] * lax.slice_in_dim(
            values, tap_index, tap_index + extent, axis=axis_id
        )
    return summed


def element_disp(node_field):
    size_x = node_field.shape[1] - 1
    size_y = node_field.shape[2] - 1
    size_z = node_field.shape[3] - 1
    corners = []
    for corner in range(8):
        off_x, off_y, off_z = (corner // 4, corner // 2 % 2, corner % 2)
        corners.append(
            node_field[:, off_x : off_x + size_x, off_y : off_y + size_y, off_z : off_z + size_z]
        )
    return jnp.stack(corners).reshape(24, size_x, size_y, size_z)


def element_forces(node_field, modulus, stiffness):
    local_disp = element_disp(node_field)
    local_force = jnp.einsum("ij,jabc->iabc", stiffness, local_disp, precision=highest) * modulus
    local_force = local_force.reshape((8, 3) + modulus.shape)
    summed = jnp.zeros_like(node_field)
    for corner in range(8):
        off_x, off_y, off_z = (corner // 4, corner // 2 % 2, corner % 2)
        summed = summed + jnp.pad(
            local_force[corner],
            ((0, 0), (off_x, 1 - off_x), (off_y, 1 - off_y), (off_z, 1 - off_z)),
        )
    return summed


def element_energy(node_field, stiffness):
    local_disp = element_disp(node_field)
    local_force = jnp.einsum("ij,jabc->iabc", stiffness, local_disp, precision=highest)
    return jnp.sum(local_disp * local_force, axis=0)


def local_gram(left_field, right_field):
    return jnp.einsum("iabcd,jabcd->ij", left_field, right_field, precision=highest)


def global_gram(left_field, right_field):
    return lax.psum(local_gram(left_field, right_field), ("gx", "gy"))


def mix_cases(field, coeffs):
    return jnp.einsum("kabcd,kj->jabcd", field, coeffs, precision=highest)


def solve_spd(matrix, rhs_matrix):
    factor = jnp.linalg.cholesky(matrix)
    matrix_order = matrix.shape[0]
    forward = []
    for row_index in range(matrix_order):
        partial_sum = rhs_matrix[row_index]
        for col_index in range(row_index):
            partial_sum = partial_sum - factor[row_index, col_index] * forward[col_index]
        forward.append(partial_sum / factor[row_index, row_index])
    backward = [None] * matrix_order
    for row_index in reversed(range(matrix_order)):
        partial_sum = forward[row_index]
        for col_index in range(row_index + 1, matrix_order):
            partial_sum = partial_sum - factor[col_index, row_index] * backward[col_index]
        backward[row_index] = partial_sum / factor[row_index, row_index]
    return jnp.stack(backward)


def pad_upper_z(field):
    return jnp.pad(field, ((0, 0), (0, 0), (0, 0), (0, 0), (0, 1)))


def gather_upper(field):
    from_x = from_behind(field[:, :, :1], "gx", -1)
    widened = jnp.concatenate([field, from_x], axis=2)
    from_y = from_behind(widened[:, :, :, :1], "gy", -1)
    return jnp.concatenate([widened, from_y], axis=3)


def return_lower(forces):
    size_x = forces.shape[2] - 1
    size_y = forces.shape[3] - 1
    to_y = from_behind(forces[:, :, :, size_y:], "gy", 1)
    kept = forces[:, :, :, :size_y]
    kept = jnp.concatenate([kept[:, :, :, :1] + to_y, kept[:, :, :, 1:]], axis=3)
    to_x = from_behind(kept[:, :, size_x:], "gx", 1)
    kept = kept[:, :, :size_x]
    return jnp.concatenate([kept[:, :, :1] + to_x, kept[:, :, 1:]], axis=2)


def on_device(start_disp, bone_mask, density, load_nodes, load_forces):
    stiffness = jnp.asarray(hex_stiffness(), jnp.float32)
    modulus = bone_mask.astype(jnp.float32) * density * density
    case_count = start_disp.shape[0]
    size_x = start_disp.shape[2]
    size_y = start_disp.shape[3]
    size_z = start_disp.shape[4]

    def apply_operator(field):
        node_field = pad_upper_z(gather_upper(field))
        forces = lax.map(
            lambda case_field: element_forces(case_field, modulus, stiffness), node_field
        )
        return return_lower(forces[..., :-1]) + spring * field

    slot_ids = jnp.arange(size_x * size_y, dtype=jnp.int32)
    matches = (load_nodes[0, 0][:, :, None] == slot_ids).astype(jnp.float32)
    top_plane = jnp.einsum("cls,ckl->cks", matches, load_forces[0, 0], precision=highest).reshape(
        case_count, 3, size_x, size_y
    )
    applied = apply_operator(start_disp)
    residual = jnp.concatenate(
        [-applied[..., :-1], (top_plane - applied[..., -1])[..., None]], axis=4
    )
    solution = start_disp
    norm_now = global_gram(residual, residual)
    applied = apply_operator(residual)
    step_alpha = solve_spd(global_gram(residual, applied), norm_now)
    solution = solution + mix_cases(residual, step_alpha)
    node_field = pad_upper_z(gather_upper(solution))
    energy = jnp.sum(
        lax.map(lambda case_field: element_energy(case_field, stiffness), node_field), axis=0
    )
    stimulus = modulus * energy
    smooth = blur_valid(with_halo(stimulus, (("gx", 0),), 4), 0, size_x)
    smooth = blur_valid(with_halo(smooth, (("gy", 1),), 4), 1, size_y)
    smooth = blur_valid(jnp.pad(smooth, ((0, 0), (0, 0), (4, 4))), 2, size_z)
    summed = lax.psum(jnp.sum(smooth), ("gx", "gy"))
    mean_stim = summed / (size_x * size_y * size_z * lax.axis_size("gx") * lax.axis_size("gy"))
    new_density = jnp.minimum(density * (0.5 + 0.5 * smooth / (mean_stim + mean_eps)), density_cap)
    return (solution, new_density)


def solution(mesh):
    return jax.shard_map(
        on_device,
        mesh=mesh,
        in_specs=(
            P(None, None, "gx", "gy", None),
            P("gx", "gy", None),
            P("gx", "gy", None),
            P("gx", "gy", None, None),
            P("gx", "gy", None, None, None),
        ),
        out_specs=(P(None, None, "gx", "gy", None), P("gx", "gy", None)),
        check_vma=False,
    )
```

profile of v0, /device:TPU:1, one launch (start us, length us, event | category | flops | bytes accessed | tf_op | source)
XLA Modules:
  0.0 417.8 jit_solution(12601050354318549686)
XLA Ops:
  0.6 0.9 slice.505
  1.5 1.3 collective-permute-start
  2.8 1.0 constant_dynamic-update-slice_fusion.1
  3.8 4.3 %collective-permute-done = f32[6,3,1,8,128]{4,3,2,1,0:T(8,128)S(1)} collective-permute-done((f32[6,3,1,8,128]{4,3,2,1,0:T(8,128)S(1)}, f32[6,3,1,8,128]{4,3,2,1,0:T(8,128)S(1)}, u32[]{:S(2)}, u32[]{:S(2)}) %collective-permute-start) | collective-permute-done | bytes 73760 | tf_op jit(solution)/shard_map/ppermute | solution.py:18
  8.1 8.5 %collective-permute-start.1 = (f32[6,3,5,1,128]{4,3,2,1,0:T(1,128)S(1)}, f32[6,3,5,1,128]{4,3,2,1,0:T(1,128)S(1)}, u32[]{:S(2)}, u32[]{:S(2)}) collective-permute-start(f32[6,3,5,1,128]{4,3,2,1,0:T(1,128)S(1)} %slice.696), channel_id=1, source_target_pairs={{1,0},{2,1},{3,2},{4,3},{5,4},{6,5},{7,6},{8,7},{9,8},{10,9},{11,1... | collective-permute-start | bytes 138248 | tf_op jit(solution)/shard_map/ppermute | solution.py:18
  16.6 0.7 multiply_multiply_fusion
  18.0 46.3 %while.37 = (s32[]{:T(128)}, f32[6,3,5,9,129]{4,0,3,2,1:T(8,128)S(1)}, f32[6,3,5,9,129]{4,3,2,1,0:T(8,128)S(1)}, f32[4,8,128]{2,1,0:T(8,128)S(1)}, s32[]{:T(128)}, /*index=5*/f32[24,24,1,1]{1,0,3,2:T(8,128)S(1)}, s32[]{:T(128)}) while((s32[]{:T(128)}, f32[6,3,5,9,129]{4,0,3,2,1:T(8,128)S(1)}, ...), condition=%wide.region_1.2_spmd.clone, body=%wide.region_0.1_spmd.sunk.clone.sunk | while | flops 28531760 | bytes 3258905 | solution.py:188
  18.4 0.7 fusion.163
  19.8 5.9 %dynamic_update_slice.27 = f32[6,3,5,9,129]{4,0,3,2,1:T(8,128)S(1)} dynamic-update-slice(f32[6,3,5,9,129]{4,0,3,2,1:T(8,128)S(1)} %get-tuple-element.402, f32[1,3,5,9,129]{4,0,3,2,1:T(1,128)S(1)} %copy.116, s32[]{:T(128)} %get-tuple-element.401, s32[]{:T(128)} %constant.103.clone.1..sunk, s32[]{:T(128)} %constant.103.clone.1..sunk, s32[]{:T(128)} %constant.103.clone.1..sunk, s32[]{:T(128)} %constant.103.clone.1..sunk) | dynamic-update-slice | bytes 139324 | tf_op jit(solution)/shard_map/while/body/jit(dynamic_update_index_in_dim)/dynamic_update_slice | solution.py:188
  26.2 0.7 fusion.163
  27.5 5.9 %dynamic_update_slice.27 = f32[6,3,5,9,129]{4,0,3,2,1:T(8,128)S(1)} dynamic-update-slice(f32[6,3,5,9,129]{4,0,3,2,1:T(8,128)S(1)} %get-tuple-element.402, f32[1,3,5,9,129]{4,0,3,2,1:T(1,128)S(1)} %copy.116, s32[]{:T(128)} %get-tuple-element.401, s32[]{:T(128)} %constant.103.clone.1..sunk, s32[]{:T(128)} %constant.103.clone.1..sunk, s32[]{:T(128)} %constant.103.clone.1..sunk, s32[]{:T(128)} %constant.103.clone.1..sunk) | dynamic-update-slice | bytes 139324 | tf_op jit(solution)/shard_map/while/body/jit(dynamic_update_index_in_dim)/dynamic_update_slice | solution.py:188
  33.9 0.7 fusion.163
  35.2 5.9 %dynamic_update_slice.27 = f32[6,3,5,9,129]{4,0,3,2,1:T(8,128)S(1)} dynamic-update-slice(f32[6,3,5,9,129]{4,0,3,2,1:T(8,128)S(1)} %get-tuple-element.402, f32[1,3,5,9,129]{4,0,3,2,1:T(1,128)S(1)} %copy.116, s32[]{:T(128)} %get-tuple-element.401, s32[]{:T(128)} %constant.103.clone.1..sunk, s32[]{:T(128)} %constant.103.clone.1..sunk, s32[]{:T(128)} %constant.103.clone.1..sunk, s32[]{:T(128)} %constant.103.clone.1..sunk) | dynamic-update-slice | bytes 139324 | tf_op jit(solution)/shard_map/while/body/jit(dynamic_update_index_in_dim)/dynamic_update_slice | solution.py:188
  41.6 0.7 fusion.163
  42.9 5.9 %dynamic_update_slice.27 = f32[6,3,5,9,129]{4,0,3,2,1:T(8,128)S(1)} dynamic-update-slice(f32[6,3,5,9,129]{4,0,3,2,1:T(8,128)S(1)} %get-tuple-element.402, f32[1,3,5,9,129]{4,0,3,2,1:T(1,128)S(1)} %copy.116, s32[]{:T(128)} %get-tuple-element.401, s32[]{:T(128)} %constant.103.clone.1..sunk, s32[]{:T(128)} %constant.103.clone.1..sunk, s32[]{:T(128)} %constant.103.clone.1..sunk, s32[]{:T(128)} %constant.103.clone.1..sunk) | dynamic-update-slice | bytes 139324 | tf_op jit(solution)/shard_map/while/body/jit(dynamic_update_index_in_dim)/dynamic_update_slice | solution.py:188
  49.3 0.7 fusion.163
  50.6 5.9 %dynamic_update_slice.27 = f32[6,3,5,9,129]{4,0,3,2,1:T(8,128)S(1)} dynamic-update-slice(f32[6,3,5,9,129]{4,0,3,2,1:T(8,128)S(1)} %get-tuple-element.402, f32[1,3,5,9,129]{4,0,3,2,1:T(1,128)S(1)} %copy.116, s32[]{:T(128)} %get-tuple-element.401, s32[]{:T(128)} %constant.103.clone.1..sunk, s32[]{:T(128)} %constant.103.clone.1..sunk, s32[]{:T(128)} %constant.103.clone.1..sunk, s32[]{:T(128)} %constant.103.clone.1..sunk) | dynamic-update-slice | bytes 139324 | tf_op jit(solution)/shard_map/while/body/jit(dynamic_update_index_in_dim)/dynamic_update_slice | solution.py:188
  58.3 5.9 %dynamic_update_slice.27 = f32[6,3,5,9,129]{4,0,3,2,1:T(8,128)S(1)} dynamic-update-slice(f32[6,3,5,9,129]{4,0,3,2,1:T(8,128)S(1)} %get-tuple-element.402, f32[1,3,5,9,129]{4,0,3,2,1:T(1,128)S(1)} %copy.116, s32[]{:T(128)} %get-tuple-element.401, s32[]{:T(128)} %constant.103.clone.1..sunk, s32[]{:T(128)} %constant.103.clone.1..sunk, s32[]{:T(128)} %constant.103.clone.1..sunk, s32[]{:T(128)} %constant.103.clone.1..sunk) | dynamic-update-slice | bytes 139324 | tf_op jit(solution)/shard_map/while/body/jit(dynamic_update_index_in_dim)/dynamic_update_slice | solution.py:188
  64.3 1.9 collective-permute-start.2
  66.3 1.2 collective-permute-done.2
  67.6 1.3 collective-permute-start.3
  69.7 1.3 collective-permute-done.3
  71.6 1.3 collective-permute-start.4
  72.9 4.8 %collective-permute-done.4 = f32[6,3,1,8,128]{4,0,3,2,1:T(8,128)S(1)} collective-permute-done((f32[6,3,1,8,128]{4,0,3,2,1:T(8,128)S(1)}, f32[6,3,1,8,128]{4,0,3,2,1:T(8,128)S(1)}, u32[]{:S(2)}, u32[]{:S(2)}) %collective-permute-start.4) | collective-permute-done | bytes 73760 | tf_op jit(solution)/shard_map/ppermute | solution.py:18
  77.8 3.6 collective-permute-start.5
  81.4 3.6 collective-permute-done.5
  85.3 47.1 %while.38 = (s32[]{:T(128)}, f32[6,3,5,9,129]{4,0,3,2,1:T(8,128)S(1)}, f32[6,3,5,9,129]{4,0,3,2,1:T(8,128)S(1)}, f32[4,8,128]{2,1,0:T(8,128)S(1)}, s32[]{:T(128)}, /*index=5*/f32[24,24,1,1]{1,0,3,2:T(8,128)S(1)}, s32[]{:T(128)}) while((s32[]{:T(128)}, f32[6,3,5,9,129]{4,0,3,2,1:T(8,128)S(1)}, ...), condition=%wide.region_4.5_spmd.clone, body=%wide.region_3.4_spmd.sunk.clone.sunk | while | flops 28531760 | bytes 3398225 | solution.py:188
  87.2 5.9 %dynamic_update_slice.28 = f32[6,3,5,9,129]{4,0,3,2,1:T(8,128)S(1)} dynamic-update-slice(f32[6,3,5,9,129]{4,0,3,2,1:T(8,128)S(1)} %get-tuple-element.423, f32[1,3,5,9,129]{4,0,3,2,1:T(1,128)S(1)} %copy.119, s32[]{:T(128)} %get-tuple-element.422, s32[]{:T(128)} %constant.103.clone.1..sunk.1, s32[]{:T(128)} %constant.103.clone.1..sunk.1, s32[]{:T(128)} %constant.103.clone.1..sunk.1, ...) | dynamic-update-slice | bytes 139324 | tf_op jit(solution)/shard_map/while/body/jit(dynamic_update_index_in_dim)/dynamic_update_slice | solution.py:188
  95.1 5.9 %dynamic_update_slice.28 = f32[6,3,5,9,129]{4,0,3,2,1:T(8,128)S(1)} dynamic-update-slice(f32[6,3,5,9,129]{4,0,3,2,1:T(8,128)S(1)} %get-tuple-element.423, f32[1,3,5,9,129]{4,0,3,2,1:T(1,128)S(1)} %copy.119, s32[]{:T(128)} %get-tuple-element.422, s32[]{:T(128)} %constant.103.clone.1..sunk.1, s32[]{:T(128)} %constant.103.clone.1..sunk.1, s32[]{:T(128)} %constant.103.clone.1..sunk.1, ...) | dynamic-update-slice | bytes 139324 | tf_op jit(solution)/shard_map/while/body/jit(dynamic_update_index_in_dim)/dynamic_update_slice | solution.py:188
  102.9 5.9 %dynamic_update_slice.28 = f32[6,3,5,9,129]{4,0,3,2,1:T(8,128)S(1)} dynamic-update-slice(f32[6,3,5,9,129]{4,0,3,2,1:T(8,128)S(1)} %get-tuple-element.423, f32[1,3,5,9,129]{4,0,3,2,1:T(1,128)S(1)} %copy.119, s32[]{:T(128)} %get-tuple-element.422, s32[]{:T(128)} %constant.103.clone.1..sunk.1, s32[]{:T(128)} %constant.103.clone.1..sunk.1, s32[]{:T(128)} %constant.103.clone.1..sunk.1, ...) | dynamic-update-slice | bytes 139324 | tf_op jit(solution)/shard_map/while/body/jit(dynamic_update_index_in_dim)/dynamic_update_slice | solution.py:188
  110.7 5.9 %dynamic_update_slice.28 = f32[6,3,5,9,129]{4,0,3,2,1:T(8,128)S(1)} dynamic-update-slice(f32[6,3,5,9,129]{4,0,3,2,1:T(8,128)S(1)} %get-tuple-element.423, f32[1,3,5,9,129]{4,0,3,2,1:T(1,128)S(1)} %copy.119, s32[]{:T(128)} %get-tuple-element.422, s32[]{:T(128)} %constant.103.clone.1..sunk.1, s32[]{:T(128)} %constant.103.clone.1..sunk.1, s32[]{:T(128)} %constant.103.clone.1..sunk.1, ...) | dynamic-update-slice | bytes 139324 | tf_op jit(solution)/shard_map/while/body/jit(dynamic_update_index_in_dim)/dynamic_update_slice | solution.py:188
  118.6 5.9 %dynamic_update_slice.28 = f32[6,3,5,9,129]{4,0,3,2,1:T(8,128)S(1)} dynamic-update-slice(f32[6,3,5,9,129]{4,0,3,2,1:T(8,128)S(1)} %get-tuple-element.423, f32[1,3,5,9,129]{4,0,3,2,1:T(1,128)S(1)} %copy.119, s32[]{:T(128)} %get-tuple-element.422, s32[]{:T(128)} %constant.103.clone.1..sunk.1, s32[]{:T(128)} %constant.103.clone.1..sunk.1, s32[]{:T(128)} %constant.103.clone.1..sunk.1, ...) | dynamic-update-slice | bytes 139324 | tf_op jit(solution)/shard_map/while/body/jit(dynamic_update_index_in_dim)/dynamic_update_slice | solution.py:188
  126.4 5.9 %dynamic_update_slice.28 = f32[6,3,5,9,129]{4,0,3,2,1:T(8,128)S(1)} dynamic-update-slice(f32[6,3,5,9,129]{4,0,3,2,1:T(8,128)S(1)} %get-tuple-element.423, f32[1,3,5,9,129]{4,0,3,2,1:T(1,128)S(1)} %copy.119, s32[]{:T(128)} %get-tuple-element.422, s32[]{:T(128)} %constant.103.clone.1..sunk.1, s32[]{:T(128)} %constant.103.clone.1..sunk.1, s32[]{:T(128)} %constant.103.clone.1..sunk.1, ...) | dynamic-update-slice | bytes 139324 | tf_op jit(solution)/shard_map/while/body/jit(dynamic_update_index_in_dim)/dynamic_update_slice | solution.py:188
  132.4 1.9 collective-permute-start.6
  134.4 1.2 collective-permute-done.6
  135.6 4.7 %collective-permute-start.7 = (f32[6,3,1,8,128]{4,0,3,2,1:T(8,128)S(1)}, f32[6,3,1,8,128]{4,0,3,2,1:T(8,128)S(1)}, u32[]{:S(2)}, u32[]{:S(2)}) collective-permute-start(f32[6,3,1,8,128]{4,0,3,2,1:T(8,128)S(1)} %pad_maximum_fusion.1), channel_id=1, source_target_pairs={{0,16},{16,32},{32,48},{48,64},{64,80},{80,96},{96,112},{112,128},... | collective-permute-start | bytes 221192 | tf_op jit(solution)/shard_map/ppermute | solution.py:18
  140.3 1.1 convolution_bitcast_fusion.2
  141.4 1.0 collective-permute-done.7
  142.4 1.1 convolution_bitcast_fusion.1
  143.5 108.2 %all-reduce.20 = (f32[6,6]{1,0:T(8,128)S(1)}, f32[6,6]{0,1:T(8,128)S(1)}) all-reduce(f32[6,6]{1,0:T(8,128)S(1)} %convolution_bitcast_fusion.2, f32[6,6]{0,1:T(8,128)S(1)} %convolution_bitcast_fusion.1), channel_id=1, replica_groups=mesh['gx'=32,'gy'=16] {'gx','gy'}, use_global_device_ids=true, to_apply=%region_2.3 | all-reduce | flops 72 | bytes 576 | tf_op jit(solution)/shard_map/psum | solution.py:131
  253.7 0.7 fusion.113
  256.3 9.5 %subtract_divide_fusion.6 = (f32[1,6]{1,0:T(1,128)S(1)}, f32[1,6]{1,0:T(1,128)S(1)}, f32[1,6]{1,0:T(1,128)S(1)}, f32[1,6]{1,0:T(1,128)S(1)}, f32[1,6]{1,0:T(1,128)S(1)}) fusion(f32[6,6]{1,0:T(8,128)S(1)} %get-tuple-element.239, f32[]{:T(128)} %bitcast.19, f32[]{:T(128)} %bitcast.18, f32[]{:T(128)} %bitcast.17, f32[]{:T(128)} %bitcast.16, f32[]{:T(128)} %bitcast.15, ...), kind=kLoop, calls=%fused_computation.219 | loop fusion | flops 150 | bytes 300 | tf_op jit(solution)/shard_map/div | solution.py:146
  265.8 12.6 %subtract_divide_fusion = (f32[1,6]{1,0:T(1,128)S(1)}, f32[1,6]{1,0:T(1,128)S(1)}, f32[1,6]{1,0:T(1,128)S(1)}, f32[1,6]{1,0:T(1,128)S(1)}, f32[1,6]{1,0:T(1,128)S(1)}, /*index=5*/f32[1,6]{1,0:T(1,128)S(1)}) fusion(f32[1,6]{1,0:T(1,128)S(1)} %get-tuple-element.253, f32[]{:T(128)} %bitcast.21, f32[]{:T(128)} %bitcast.16, f32[]{:T(128)} %bitcast.12, ...), kind=kLoop, calls=%fused_computation.213 | loop fusion | flops 276 | bytes 372 | tf_op jit(solution)/shard_map/div | solution.py:152
  278.4 0.8 convolution_add_fusion
  279.3 1.3 collective-permute-start.8
  280.6 4.1 collective-permute-done.8
  284.6 3.7 collective-permute-start.9
  288.4 3.8 collective-permute-done.9
  292.3 8.5 %while.39 = (s32[]{:T(128)}, f32[6,4,8,128]{3,2,1,0:T(8,128)S(1)}, f32[6,3,5,9,129]{4,0,3,2,1:T(8,128)S(1)}, s32[]{:T(128)}, f32[24,24,1,1]{1,0,3,2:T(8,128)S(1)}) while((s32[]{:T(128)}, f32[6,4,8,128]{3,2,1,0:T(8,128)S(1)}, f32[6,3,5,9,129]{4,0,3,2,1:T(8,128)S(1)}, s32[]{:T(128)}, f32[24,24,1,1]{1,0,3,2:T(8,128)S(1)}) %tuple.141), condition=%wide.region_10.11_spmd.clone, body=%wide.region_8.10_spmd.sunk.clone.sunk | while | flops 28504064 | bytes 1509813 | solution.py:209
  292.8 0.8 fusion.187
  294.2 0.8 fusion.187
  295.7 0.8 fusion.187
  297.1 0.8 fusion.187
  298.5 0.8 fusion.187
  299.9 0.8 fusion.187
  300.8 1.3 collective-permute-start.10
  302.1 1.3 collective-permute-start.11
  303.5 3.4 collective-permute-done.11
  306.9 3.0 collective-permute-start.12
  309.9 1.9 collective-permute-start.13
  311.9 0.8 copy.64
  312.6 2.3 collective-permute-done.13
  315.0 0.7 fusion.108
  315.7 100.9 %psum.23 = f32[]{:T(128)} all-reduce(f32[]{:T(128)} %get-tuple-element.241), channel_id=1, replica_groups=mesh['gx'=32,'gy'=16] {'gx','gy'}, use_global_device_ids=true, to_apply=%region_13.14 | all-reduce | flops 1 | bytes 8 | tf_op jit(solution)/shard_map/psum | solution.py:215
  (279 shorter events, 26.4 us)
Async XLA Ops:
  1.5 6.6 %collective-permute-start = (f32[6,3,1,8,128]{4,3,2,1,0:T(8,128)S(1)}, f32[6,3,1,8,128]{4,3,2,1,0:T(8,128)S(1)}, u32[]{:S(2)}, u32[]{:S(2)}) collective-permute-start(f32[6,3,1,8,128]{4,3,2,1,0:T(8,128)S(1)} %slice.505), channel_id=1, source_target_pairs={{16,0},{32,16},{48,32},{64,48},{80,64},{96,80},{112,96},{128,112},... | collective-permute-start | bytes 221192 | tf_op jit(solution)/shard_map/ppermute | solution.py:18
  8.1 9.3 %collective-permute-start.1 = (f32[6,3,5,1,128]{4,3,2,1,0:T(1,128)S(1)}, f32[6,3,5,1,128]{4,3,2,1,0:T(1,128)S(1)}, u32[]{:S(2)}, u32[]{:S(2)}) collective-permute-start(f32[6,3,5,1,128]{4,3,2,1,0:T(1,128)S(1)} %slice.696), channel_id=1, source_target_pairs={{1,0},{2,1},{3,2},{4,3},{5,4},{6,5},{7,6},{8,7},{9,8},{10,9},{11,1... | collective-permute-start | bytes 138248 | tf_op jit(solution)/shard_map/ppermute | solution.py:18
  17.3 0.7 copy-start.1
  18.0 48.2 %copy-start.3 = (s32[1,1,6,32]{3,1,2,0:T(1,128)S(1)}, s32[1,1,6,32]{3,1,2,0:T(1,128)}, u32[]{:S(2)}) copy-start(s32[1,1,6,32]{3,1,2,0:T(1,128)} %param.15) | copy-start | bytes 2308
  64.3 4.6 %copy-start.4 = (f32[1,1,6,3,32]{4,1,3,2,0:T(1,128)S(1)}, f32[1,1,6,3,32]{4,1,3,2,0:T(1,128)}, u32[]{:S(2)}) copy-start(f32[1,1,6,3,32]{4,1,3,2,0:T(1,128)} %param.16) | copy-start | bytes 6916
  64.3 3.2 collective-permute-start.2
  66.3 4.7 %copy-start = (f32[6,3,4,8,128]{4,3,2,1,0:T(8,128)S(1)}, f32[6,3,4,8,128]{4,3,2,1,0:T(8,128)}, u32[]{:S(2)}) copy-start(f32[6,3,4,8,128]{4,3,2,1,0:T(8,128)} %param.12) | copy-start | bytes 884740
  67.6 3.4 collective-permute-start.3
  71.6 6.1 %collective-permute-start.4 = (f32[6,3,1,8,128]{4,0,3,2,1:T(8,128)S(1)}, f32[6,3,1,8,128]{4,0,3,2,1:T(8,128)S(1)}, u32[]{:S(2)}, u32[]{:S(2)}) collective-permute-start(f32[6,3,1,8,128]{4,0,3,2,1:T(8,128)S(1)} %fusion.43), channel_id=1, source_target_pairs={{16,0},{32,16},{48,32},{64,48},{80,64},{96,80},{112,96},{128,112},... | collective-permute-start | bytes 221192 | tf_op jit(solution)/shard_map/ppermute | solution.py:18
  77.8 7.3 %collective-permute-start.5 = (f32[6,3,5,1,128]{4,0,3,2,1:T(8,128)S(1)}, f32[6,3,5,1,128]{4,0,3,2,1:T(8,128)S(1)}, u32[]{:S(2)}, u32[]{:S(2)}) collective-permute-start(f32[6,3,5,1,128]{4,0,3,2,1:T(8,128)S(1)} %pad_maximum_fusion.4), channel_id=1, source_target_pairs={{1,0},{2,1},{3,2},{4,3},{5,4},{6,5},{7,6},{8,7},{9,8},{10,9},{11,1... | collective-permute-start | bytes 138248 | tf_op jit(solution)/shard_map/ppermute | solution.py:18
  132.4 3.2 collective-permute-start.6
  135.6 6.8 %collective-permute-start.7 = (f32[6,3,1,8,128]{4,0,3,2,1:T(8,128)S(1)}, f32[6,3,1,8,128]{4,0,3,2,1:T(8,128)S(1)}, u32[]{:S(2)}, u32[]{:S(2)}) collective-permute-start(f32[6,3,1,8,128]{4,0,3,2,1:T(8,128)S(1)} %pad_maximum_fusion.1), channel_id=1, source_target_pairs={{0,16},{16,32},{32,48},{48,64},{64,80},{80,96},{96,112},{112,128},... | collective-permute-start | bytes 221192 | tf_op jit(solution)/shard_map/ppermute | solution.py:18
  279.3 5.4 %collective-permute-start.8 = (f32[6,3,1,8,128]{4,0,3,2,1:T(8,128)S(1)}, f32[6,3,1,8,128]{4,0,3,2,1:T(8,128)S(1)}, u32[]{:S(2)}, u32[]{:S(2)}) collective-permute-start(f32[6,3,1,8,128]{4,0,3,2,1:T(8,128)S(1)} %slice.701), channel_id=1, source_target_pairs={{16,0},{32,16},{48,32},{64,48},{80,64},{96,80},{112,96},{128,112},... | collective-permute-start | bytes 221192 | tf_op jit(solution)/shard_map/ppermute | solution.py:18
  284.6 7.5 %collective-permute-start.9 = (f32[6,3,5,1,128]{4,0,3,2,1:T(8,128)S(1)}, f32[6,3,5,1,128]{4,0,3,2,1:T(8,128)S(1)}, u32[]{:S(2)}, u32[]{:S(2)}) collective-permute-start(f32[6,3,5,1,128]{4,0,3,2,1:T(8,128)S(1)} %pad_maximum_fusion.3), channel_id=1, source_target_pairs={{1,0},{2,1},{3,2},{4,3},{5,4},{6,5},{7,6},{8,7},{9,8},{10,9},{11,1... | collective-permute-start | bytes 138248 | tf_op jit(solution)/shard_map/ppermute | solution.py:18
  292.3 124.9 %copy-start.2 = (f32[4,8,128]{2,1,0:T(8,128)S(1)}, f32[4,8,128]{2,1,0:T(8,128)}, u32[]{:S(2)}) copy-start(f32[4,8,128]{2,1,0:T(8,128)} %param.14) | copy-start | bytes 49156
  300.8 2.6 collective-permute-start.10
  302.1 4.7 %collective-permute-start.11 = (f32[4,8,128]{2,1,0:T(8,128)S(1)}, f32[4,8,128]{2,1,0:T(8,128)S(1)}, u32[]{:S(2)}, u32[]{:S(2)}) collective-permute-start(f32[4,8,128]{2,1,0:T(8,128)S(1)} %mul.463), channel_id=1, source_target_pairs={{16,0},{32,16},{48,32},{64,48},{80,64},{96,80},{112,96},{128,112},... | collective-permute-start | bytes 49160 | tf_op jit(solution)/shard_map/ppermute | solution.py:31
  306.9 5.7 %collective-permute-start.12 = (f32[4,4,128]{2,1,0:T(4,128)S(1)}, f32[4,4,128]{2,1,0:T(4,128)S(1)}, u32[]{:S(2)}, u32[]{:S(2)}) collective-permute-start(f32[4,4,128]{2,1,0:T(4,128)S(1)} %get-tuple-element.270), channel_id=1, source_target_pairs={{0,1},{1,2},{2,3},{3,4},{4,5},{5,6},{6,7},{7,8},{8,9},{9,10},{10,1... | collective-permute-start | bytes 24584 | tf_op jit(solution)/shard_map/ppermute | solution.py:29
  309.9 5.0 %collective-permute-start.13 = (f32[4,4,128]{2,1,0:T(4,128)S(1)}, f32[4,4,128]{2,1,0:T(4,128)S(1)}, u32[]{:S(2)}, u32[]{:S(2)}) collective-permute-start(f32[4,4,128]{2,1,0:T(4,128)S(1)} %get-tuple-element.271), channel_id=1, source_target_pairs={{1,0},{2,1},{3,2},{4,3},{5,4},{6,5},{7,6},{8,7},{9,8},{10,9},{11,1... | collective-permute-start | bytes 24584 | tf_op jit(solution)/shard_map/ppermute | solution.py:31
where the time goes:
time: 419 us; the launch traced here: 418 us
  blocking collectives  209 us (50%)
  local copies, waits for them, and re-layouts  88.3 us (21%)
  starting transfers between devices  37.1 us (9%)
  other arithmetic  31.3 us (7%)
  waiting for transfers between devices  31.1 us (7%)
  matrix products  16.5 us (4%)
    psum x1, blocking collectives, global_gram(): return lax.psum(local_gram(left_field, right_field), ('gx', 'gy'))  108 us
    psum x1, blocking collectives, on_device(): summed = lax.psum(jnp.sum(smooth), ('gx', 'gy'))  101 us
    dynamic_update_slice x24, local copies, waits for them, and re-layouts, apply_operator(): lax.map(lambda case_field: element_forces(case_field, modulus, stiffness)...  73.1 us
    ppermute x10, starting transfers between devices, from_behind(): return lax.ppermute(block, axis, route)  29.5 us
    ppermute x10, waiting for transfers between devices, from_behind(): return lax.ppermute(block, axis, route)  25.4 us
    div x1, other arithmetic, solve_spd(): backward[row_index] = partial_sum / factor[row_index, row_index]  12.6 us
    div x1, other arithmetic, solve_spd(): forward.append(partial_sum / factor[row_index, row_index])  9.49 us
  transfers between devices with their start and end apart: 14, of which 12 were waited for; matrix products, arithmetic and copies ran while one was open for 1% of the time, Pallas kernels for 0%

commit v1 on v0

--- a/solution.py
+++ b/solution.py
@@ -128,7 +128,7 @@
 
 
 def global_gram(left_field, right_field):
-    return lax.psum(local_gram(left_field, right_field), ("gx", "gy"))
+    return lax.psum(lax.psum(local_gram(left_field, right_field), "gx"), "gy")
 
 
 def mix_cases(field, coeffs):

time: 419 us -> 412 us (0.983)
  blocking collectives: 209 us -> 203 us
    psum x1 -> x2, blocking collectives: 108 us -> 104 us  [global_gram(): return lax.psum(lax.psum(local_gram(left_field, right_field), 'gx'), 'gy')]
where the time goes in v1:
time: 412 us; the launch traced here: 410 us
  blocking collectives  203 us (49%)
  local copies, waits for them, and re-layouts  88.2 us (21%)
  starting transfers between devices  36.4 us (9%)
  other arithmetic  31.1 us (8%)
  waiting for transfers between devices  30.5 us (7%)
  matrix products  16.5 us (4%)
    psum x2, blocking collectives, global_gram(): return lax.psum(lax.psum(local_gram(left_field, right_field), 'gx'), 'gy')  104 us
    psum x1, blocking collectives, on_device(): summed = lax.psum(jnp.sum(smooth), ('gx', 'gy'))  98.6 us
    dynamic_update_slice x24, local copies, waits for them, and re-layouts, apply_operator(): lax.map(lambda case_field: element_forces(case_field, modulus, stiffness)...  73.1 us
    ppermute x10, starting transfers between devices, from_behind(): return lax.ppermute(block, axis, route)  28.7 us
    ppermute x10, waiting for transfers between devices, from_behind(): return lax.ppermute(block, axis, route)  25 us
    div x1, other arithmetic, solve_spd(): backward[row_index] = partial_sum / factor[row_index, row_index]  12.6 us
    div x1, other arithmetic, solve_spd(): forward.append(partial_sum / factor[row_index, row_index])  9.36 us
    dot_general x12, matrix products, element_forces(): jnp.einsum('ij,jabc->iabc', stiffness, local_disp, precision=highest)  8.27 us
  transfers between devices with their start and end apart: 14, of which 12 were waited for; matrix products, arithmetic and copies ran while one was open for 1% of the time, Pallas kernels for 0%

profile of v1, /device:TPU:1, one launch (start us, length us, event | category | flops | bytes accessed | tf_op | source)
XLA Modules:
  0.0 409.9 jit_solution(4840381124514323695)
XLA Ops:
  0.6 0.9 slice.505
  1.5 1.3 collective-permute-start
  2.8 1.0 constant_dynamic-update-slice_fusion.1
  3.8 4.3 %collective-permute-done = f32[6,3,1,8,128]{4,3,2,1,0:T(8,128)S(1)} collective-permute-done((f32[6,3,1,8,128]{4,3,2,1,0:T(8,128)S(1)}, f32[6,3,1,8,128]{4,3,2,1,0:T(8,128)S(1)}, u32[]{:S(2)}, u32[]{:S(2)}) %collective-permute-start) | collective-permute-done | bytes 73760 | tf_op jit(solution)/shard_map/ppermute | solution.py:18
  8.1 8.5 %collective-permute-start.1 = (f32[6,3,5,1,128]{4,3,2,1,0:T(1,128)S(1)}, f32[6,3,5,1,128]{4,3,2,1,0:T(1,128)S(1)}, u32[]{:S(2)}, u32[]{:S(2)}) collective-permute-start(f32[6,3,5,1,128]{4,3,2,1,0:T(1,128)S(1)} %slice.696), channel_id=1, source_target_pairs={{1,0},{2,1},{3,2},{4,3},{5,4},{6,5},{7,6},{8,7},{9,8},{10,9},{11,1... | collective-permute-start | bytes 138248 | tf_op jit(solution)/shard_map/ppermute | solution.py:18
  16.6 0.7 multiply_multiply_fusion
  18.0 46.3 %while.37 = (s32[]{:T(128)}, f32[6,3,5,9,129]{4,0,3,2,1:T(8,128)S(1)}, f32[6,3,5,9,129]{4,3,2,1,0:T(8,128)S(1)}, f32[4,8,128]{2,1,0:T(8,128)S(1)}, s32[]{:T(128)}, /*index=5*/f32[24,24,1,1]{1,0,3,2:T(8,128)S(1)}, s32[]{:T(128)}) while((s32[]{:T(128)}, f32[6,3,5,9,129]{4,0,3,2,1:T(8,128)S(1)}, ...), condition=%wide.region_1.2_spmd.clone, body=%wide.region_0.1_spmd.sunk.clone.sunk | while | flops 28531760 | bytes 3258905 | solution.py:188
  18.4 0.7 fusion.163
  19.8 5.9 %dynamic_update_slice.27 = f32[6,3,5,9,129]{4,0,3,2,1:T(8,128)S(1)} dynamic-update-slice(f32[6,3,5,9,129]{4,0,3,2,1:T(8,128)S(1)} %get-tuple-element.404, f32[1,3,5,9,129]{4,0,3,2,1:T(1,128)S(1)} %copy.116, s32[]{:T(128)} %get-tuple-element.403, s32[]{:T(128)} %constant.103.clone.1..sunk, s32[]{:T(128)} %constant.103.clone.1..sunk, s32[]{:T(128)} %constant.103.clone.1..sunk, s32[]{:T(128)} %constant.103.clone.1..sunk) | dynamic-update-slice | bytes 139324 | tf_op jit(solution)/shard_map/while/body/jit(dynamic_update_index_in_dim)/dynamic_update_slice | solution.py:188
  26.2 0.7 fusion.163
  27.5 5.9 %dynamic_update_slice.27 = f32[6,3,5,9,129]{4,0,3,2,1:T(8,128)S(1)} dynamic-update-slice(f32[6,3,5,9,129]{4,0,3,2,1:T(8,128)S(1)} %get-tuple-element.404, f32[1,3,5,9,129]{4,0,3,2,1:T(1,128)S(1)} %copy.116, s32[]{:T(128)} %get-tuple-element.403, s32[]{:T(128)} %constant.103.clone.1..sunk, s32[]{:T(128)} %constant.103.clone.1..sunk, s32[]{:T(128)} %constant.103.clone.1..sunk, s32[]{:T(128)} %constant.103.clone.1..sunk) | dynamic-update-slice | bytes 139324 | tf_op jit(solution)/shard_map/while/body/jit(dynamic_update_index_in_dim)/dynamic_update_slice | solution.py:188
  33.9 0.7 fusion.163
  35.2 5.9 %dynamic_update_slice.27 = f32[6,3,5,9,129]{4,0,3,2,1:T(8,128)S(1)} dynamic-update-slice(f32[6,3,5,9,129]{4,0,3,2,1:T(8,128)S(1)} %get-tuple-element.404, f32[1,3,5,9,129]{4,0,3,2,1:T(1,128)S(1)} %copy.116, s32[]{:T(128)} %get-tuple-element.403, s32[]{:T(128)} %constant.103.clone.1..sunk, s32[]{:T(128)} %constant.103.clone.1..sunk, s32[]{:T(128)} %constant.103.clone.1..sunk, s32[]{:T(128)} %constant.103.clone.1..sunk) | dynamic-update-slice | bytes 139324 | tf_op jit(solution)/shard_map/while/body/jit(dynamic_update_index_in_dim)/dynamic_update_slice | solution.py:188
  41.6 0.7 fusion.163
  42.9 5.9 %dynamic_update_slice.27 = f32[6,3,5,9,129]{4,0,3,2,1:T(8,128)S(1)} dynamic-update-slice(f32[6,3,5,9,129]{4,0,3,2,1:T(8,128)S(1)} %get-tuple-element.404, f32[1,3,5,9,129]{4,0,3,2,1:T(1,128)S(1)} %copy.116, s32[]{:T(128)} %get-tuple-element.403, s32[]{:T(128)} %constant.103.clone.1..sunk, s32[]{:T(128)} %constant.103.clone.1..sunk, s32[]{:T(128)} %constant.103.clone.1..sunk, s32[]{:T(128)} %constant.103.clone.1..sunk) | dynamic-update-slice | bytes 139324 | tf_op jit(solution)/shard_map/while/body/jit(dynamic_update_index_in_dim)/dynamic_update_slice | solution.py:188
  50.6 5.9 %dynamic_update_slice.27 = f32[6,3,5,9,129]{4,0,3,2,1:T(8,128)S(1)} dynamic-update-slice(f32[6,3,5,9,129]{4,0,3,2,1:T(8,128)S(1)} %get-tuple-element.404, f32[1,3,5,9,129]{4,0,3,2,1:T(1,128)S(1)} %copy.116, s32[]{:T(128)} %get-tuple-element.403, s32[]{:T(128)} %constant.103.clone.1..sunk, s32[]{:T(128)} %constant.103.clone.1..sunk, s32[]{:T(128)} %constant.103.clone.1..sunk, s32[]{:T(128)} %constant.103.clone.1..sunk) | dynamic-update-slice | bytes 139324 | tf_op jit(solution)/shard_map/while/body/jit(dynamic_update_index_in_dim)/dynamic_update_slice | solution.py:188
  58.3 5.9 %dynamic_update_slice.27 = f32[6,3,5,9,129]{4,0,3,2,1:T(8,128)S(1)} dynamic-update-slice(f32[6,3,5,9,129]{4,0,3,2,1:T(8,128)S(1)} %get-tuple-element.404, f32[1,3,5,9,129]{4,0,3,2,1:T(1,128)S(1)} %copy.116, s32[]{:T(128)} %get-tuple-element.403, s32[]{:T(128)} %constant.103.clone.1..sunk, s32[]{:T(128)} %constant.103.clone.1..sunk, s32[]{:T(128)} %constant.103.clone.1..sunk, s32[]{:T(128)} %constant.103.clone.1..sunk) | dynamic-update-slice | bytes 139324 | tf_op jit(solution)/shard_map/while/body/jit(dynamic_update_index_in_dim)/dynamic_update_slice | solution.py:188
  64.3 1.9 collective-permute-start.2
  66.3 1.2 collective-permute-done.2
  67.6 1.3 collective-permute-start.3
  69.7 1.3 collective-permute-done.3
  71.6 1.3 collective-permute-start.4
  72.9 4.8 %collective-permute-done.4 = f32[6,3,1,8,128]{4,0,3,2,1:T(8,128)S(1)} collective-permute-done((f32[6,3,1,8,128]{4,0,3,2,1:T(8,128)S(1)}, f32[6,3,1,8,128]{4,0,3,2,1:T(8,128)S(1)}, u32[]{:S(2)}, u32[]{:S(2)}) %collective-permute-start.4) | collective-permute-done | bytes 73760 | tf_op jit(solution)/shard_map/ppermute | solution.py:18
  77.8 3.6 collective-permute-start.5
  81.4 3.6 collective-permute-done.5
  85.3 47.1 %while.38 = (s32[]{:T(128)}, f32[6,3,5,9,129]{4,0,3,2,1:T(8,128)S(1)}, f32[6,3,5,9,129]{4,0,3,2,1:T(8,128)S(1)}, f32[4,8,128]{2,1,0:T(8,128)S(1)}, s32[]{:T(128)}, /*index=5*/f32[24,24,1,1]{1,0,3,2:T(8,128)S(1)}, s32[]{:T(128)}) while((s32[]{:T(128)}, f32[6,3,5,9,129]{4,0,3,2,1:T(8,128)S(1)}, ...), condition=%wide.region_5.6_spmd.clone, body=%wide.region_4.5_spmd.sunk.clone.sunk | while | flops 28531760 | bytes 3398225 | solution.py:188
  87.2 5.9 %dynamic_update_slice.28 = f32[6,3,5,9,129]{4,0,3,2,1:T(8,128)S(1)} dynamic-update-slice(f32[6,3,5,9,129]{4,0,3,2,1:T(8,128)S(1)} %get-tuple-element.425, f32[1,3,5,9,129]{4,0,3,2,1:T(1,128)S(1)} %copy.119, s32[]{:T(128)} %get-tuple-element.424, s32[]{:T(128)} %constant.103.clone.1..sunk.1, s32[]{:T(128)} %constant.103.clone.1..sunk.1, s32[]{:T(128)} %constant.103.clone.1..sunk.1, ...) | dynamic-update-slice | bytes 139324 | tf_op jit(solution)/shard_map/while/body/jit(dynamic_update_index_in_dim)/dynamic_update_slice | solution.py:188
  95.1 5.9 %dynamic_update_slice.28 = f32[6,3,5,9,129]{4,0,3,2,1:T(8,128)S(1)} dynamic-update-slice(f32[6,3,5,9,129]{4,0,3,2,1:T(8,128)S(1)} %get-tuple-element.425, f32[1,3,5,9,129]{4,0,3,2,1:T(1,128)S(1)} %copy.119, s32[]{:T(128)} %get-tuple-element.424, s32[]{:T(128)} %constant.103.clone.1..sunk.1, s32[]{:T(128)} %constant.103.clone.1..sunk.1, s32[]{:T(128)} %constant.103.clone.1..sunk.1, ...) | dynamic-update-slice | bytes 139324 | tf_op jit(solution)/shard_map/while/body/jit(dynamic_update_index_in_dim)/dynamic_update_slice | solution.py:188
  102.9 5.9 %dynamic_update_slice.28 = f32[6,3,5,9,129]{4,0,3,2,1:T(8,128)S(1)} dynamic-update-slice(f32[6,3,5,9,129]{4,0,3,2,1:T(8,128)S(1)} %get-tuple-element.425, f32[1,3,5,9,129]{4,0,3,2,1:T(1,128)S(1)} %copy.119, s32[]{:T(128)} %get-tuple-element.424, s32[]{:T(128)} %constant.103.clone.1..sunk.1, s32[]{:T(128)} %constant.103.clone.1..sunk.1, s32[]{:T(128)} %constant.103.clone.1..sunk.1, ...) | dynamic-update-slice | bytes 139324 | tf_op jit(solution)/shard_map/while/body/jit(dynamic_update_index_in_dim)/dynamic_update_slice | solution.py:188
  110.7 5.9 %dynamic_update_slice.28 = f32[6,3,5,9,129]{4,0,3,2,1:T(8,128)S(1)} dynamic-update-slice(f32[6,3,5,9,129]{4,0,3,2,1:T(8,128)S(1)} %get-tuple-element.425, f32[1,3,5,9,129]{4,0,3,2,1:T(1,128)S(1)} %copy.119, s32[]{:T(128)} %get-tuple-element.424, s32[]{:T(128)} %constant.103.clone.1..sunk.1, s32[]{:T(128)} %constant.103.clone.1..sunk.1, s32[]{:T(128)} %constant.103.clone.1..sunk.1, ...) | dynamic-update-slice | bytes 139324 | tf_op jit(solution)/shard_map/while/body/jit(dynamic_update_index_in_dim)/dynamic_update_slice | solution.py:188
  118.6 5.9 %dynamic_update_slice.28 = f32[6,3,5,9,129]{4,0,3,2,1:T(8,128)S(1)} dynamic-update-slice(f32[6,3,5,9,129]{4,0,3,2,1:T(8,128)S(1)} %get-tuple-element.425, f32[1,3,5,9,129]{4,0,3,2,1:T(1,128)S(1)} %copy.119, s32[]{:T(128)} %get-tuple-element.424, s32[]{:T(128)} %constant.103.clone.1..sunk.1, s32[]{:T(128)} %constant.103.clone.1..sunk.1, s32[]{:T(128)} %constant.103.clone.1..sunk.1, ...) | dynamic-update-slice | bytes 139324 | tf_op jit(solution)/shard_map/while/body/jit(dynamic_update_index_in_dim)/dynamic_update_slice | solution.py:188
  126.4 5.9 %dynamic_update_slice.28 = f32[6,3,5,9,129]{4,0,3,2,1:T(8,128)S(1)} dynamic-update-slice(f32[6,3,5,9,129]{4,0,3,2,1:T(8,128)S(1)} %get-tuple-element.425, f32[1,3,5,9,129]{4,0,3,2,1:T(1,128)S(1)} %copy.119, s32[]{:T(128)} %get-tuple-element.424, s32[]{:T(128)} %constant.103.clone.1..sunk.1, s32[]{:T(128)} %constant.103.clone.1..sunk.1, s32[]{:T(128)} %constant.103.clone.1..sunk.1, ...) | dynamic-update-slice | bytes 139324 | tf_op jit(solution)/shard_map/while/body/jit(dynamic_update_index_in_dim)/dynamic_update_slice | solution.py:188
  132.4 1.9 collective-permute-start.6
  134.4 1.2 collective-permute-done.6
  135.6 4.7 %collective-permute-start.7 = (f32[6,3,1,8,128]{4,0,3,2,1:T(8,128)S(1)}, f32[6,3,1,8,128]{4,0,3,2,1:T(8,128)S(1)}, u32[]{:S(2)}, u32[]{:S(2)}) collective-permute-start(f32[6,3,1,8,128]{4,0,3,2,1:T(8,128)S(1)} %pad_maximum_fusion.1), channel_id=1, source_target_pairs={{0,16},{16,32},{32,48},{48,64},{64,80},{80,96},{96,112},{112,128},... | collective-permute-start | bytes 221192 | tf_op jit(solution)/shard_map/ppermute | solution.py:18
  140.3 1.1 convolution_bitcast_fusion.2
  141.4 1.0 collective-permute-done.7
  142.4 1.1 convolution_bitcast_fusion.1
  143.5 64.9 %all-reduce.20 = (f32[6,6]{1,0:T(8,128)S(1)}, f32[6,6]{0,1:T(8,128)S(1)}) all-reduce(f32[6,6]{1,0:T(8,128)S(1)} %convolution_bitcast_fusion.2, f32[6,6]{0,1:T(8,128)S(1)} %convolution_bitcast_fusion.1), channel_id=1, replica_groups=mesh['gx'=32,'gy'=16] {'gx'}, use_global_device_ids=true, to_apply=%region_2.3 | all-reduce | flops 72 | bytes 576 | tf_op jit(solution)/shard_map/psum | solution.py:131
  208.4 39.2 %all-reduce.21 = (f32[6,6]{1,0:T(8,128)S(1)}, f32[6,6]{0,1:T(8,128)S(1)}) all-reduce(f32[6,6]{1,0:T(8,128)S(1)} %get-tuple-element.239, f32[6,6]{0,1:T(8,128)S(1)} %get-tuple-element.240), channel_id=1, replica_groups=mesh['gx'=32,'gy'=16] {'gy'}, use_global_device_ids=true, to_apply=%region_3.4 | all-reduce | flops 72 | bytes 576 | tf_op jit(solution)/shard_map/psum | solution.py:131
  249.6 0.7 fusion.113
  252.2 9.4 %subtract_divide_fusion.6 = (f32[1,6]{1,0:T(1,128)S(1)}, f32[1,6]{1,0:T(1,128)S(1)}, f32[1,6]{1,0:T(1,128)S(1)}, f32[1,6]{1,0:T(1,128)S(1)}, f32[1,6]{1,0:T(1,128)S(1)}) fusion(f32[6,6]{1,0:T(8,128)S(1)} %get-tuple-element.241, f32[]{:T(128)} %bitcast.19, f32[]{:T(128)} %bitcast.18, f32[]{:T(128)} %bitcast.17, f32[]{:T(128)} %bitcast.16, f32[]{:T(128)} %bitcast.15, ...), kind=kLoop, calls=%fused_computation.219 | loop fusion | flops 150 | bytes 300 | tf_op jit(solution)/shard_map/div | solution.py:146
  261.6 12.6 %subtract_divide_fusion = (f32[1,6]{1,0:T(1,128)S(1)}, f32[1,6]{1,0:T(1,128)S(1)}, f32[1,6]{1,0:T(1,128)S(1)}, f32[1,6]{1,0:T(1,128)S(1)}, f32[1,6]{1,0:T(1,128)S(1)}, /*index=5*/f32[1,6]{1,0:T(1,128)S(1)}) fusion(f32[1,6]{1,0:T(1,128)S(1)} %get-tuple-element.255, f32[]{:T(128)} %bitcast.21, f32[]{:T(128)} %bitcast.16, f32[]{:T(128)} %bitcast.12, ...), kind=kLoop, calls=%fused_computation.213 | loop fusion | flops 276 | bytes 372 | tf_op jit(solution)/shard_map/div | solution.py:152
  274.2 0.8 convolution_add_fusion
  275.0 1.3 collective-permute-start.8
  276.3 4.8 %collective-permute-done.8 = f32[6,3,1,8,128]{4,0,3,2,1:T(8,128)S(1)} collective-permute-done((f32[6,3,1,8,128]{4,0,3,2,1:T(8,128)S(1)}, f32[6,3,1,8,128]{4,0,3,2,1:T(8,128)S(1)}, u32[]{:S(2)}, u32[]{:S(2)}) %collective-permute-start.8) | collective-permute-done | bytes 73760 | tf_op jit(solution)/shard_map/ppermute | solution.py:18
  281.1 2.9 collective-permute-start.9
  284.0 2.7 collective-permute-done.9
  286.8 8.5 %while.39 = (s32[]{:T(128)}, f32[6,4,8,128]{3,2,1,0:T(8,128)S(1)}, f32[6,3,5,9,129]{4,0,3,2,1:T(8,128)S(1)}, s32[]{:T(128)}, f32[24,24,1,1]{1,0,3,2:T(8,128)S(1)}) while((s32[]{:T(128)}, f32[6,4,8,128]{3,2,1,0:T(8,128)S(1)}, f32[6,3,5,9,129]{4,0,3,2,1:T(8,128)S(1)}, s32[]{:T(128)}, f32[24,24,1,1]{1,0,3,2:T(8,128)S(1)}) %tuple.141), condition=%wide.region_12.13_spmd.clone, body=%wide.region_10.12_spmd.sunk.clone.sunk | while | flops 28504064 | bytes 1509813 | solution.py:209
  287.3 0.8 fusion.187
  288.8 0.8 fusion.187
  290.2 0.8 fusion.187
  291.6 0.8 fusion.187
  293.0 0.8 fusion.187
  294.5 0.8 fusion.187
  295.4 1.3 collective-permute-start.10
  296.7 1.3 collective-permute-start.11
  298.0 3.2 collective-permute-done.11
  301.2 3.2 collective-permute-start.12
  304.4 1.9 collective-permute-start.13
  306.3 0.8 copy.64
  307.1 2.3 collective-permute-done.13
  309.4 0.7 fusion.108
  310.1 98.6 %psum.39 = f32[]{:T(128)} all-reduce(f32[]{:T(128)} %get-tuple-element.243), channel_id=1, replica_groups=mesh['gx'=32,'gy'=16] {'gx','gy'}, use_global_device_ids=true, to_apply=%region_15.16 | all-reduce | flops 1 | bytes 8 | tf_op jit(solution)/shard_map/psum | solution.py:215
  (280 shorter events, 27.1 us)
Async XLA Ops:
  1.5 6.6 %collective-permute-start = (f32[6,3,1,8,128]{4,3,2,1,0:T(8,128)S(1)}, f32[6,3,1,8,128]{4,3,2,1,0:T(8,128)S(1)}, u32[]{:S(2)}, u32[]{:S(2)}) collective-permute-start(f32[6,3,1,8,128]{4,3,2,1,0:T(8,128)S(1)} %slice.505), channel_id=1, source_target_pairs={{16,0},{32,16},{48,32},{64,48},{80,64},{96,80},{112,96},{128,112},... | collective-permute-start | bytes 221192 | tf_op jit(solution)/shard_map/ppermute | solution.py:18
  8.1 9.3 %collective-permute-start.1 = (f32[6,3,5,1,128]{4,3,2,1,0:T(1,128)S(1)}, f32[6,3,5,1,128]{4,3,2,1,0:T(1,128)S(1)}, u32[]{:S(2)}, u32[]{:S(2)}) collective-permute-start(f32[6,3,5,1,128]{4,3,2,1,0:T(1,128)S(1)} %slice.696), channel_id=1, source_target_pairs={{1,0},{2,1},{3,2},{4,3},{5,4},{6,5},{7,6},{8,7},{9,8},{10,9},{11,1... | collective-permute-start | bytes 138248 | tf_op jit(solution)/shard_map/ppermute | solution.py:18
  17.3 0.7 copy-start.1
  18.0 48.2 %copy-start.3 = (s32[1,1,6,32]{3,1,2,0:T(1,128)S(1)}, s32[1,1,6,32]{3,1,2,0:T(1,128)}, u32[]{:S(2)}) copy-start(s32[1,1,6,32]{3,1,2,0:T(1,128)} %param.15) | copy-start | bytes 2308
  64.3 4.6 %copy-start.4 = (f32[1,1,6,3,32]{4,1,3,2,0:T(1,128)S(1)}, f32[1,1,6,3,32]{4,1,3,2,0:T(1,128)}, u32[]{:S(2)}) copy-start(f32[1,1,6,3,32]{4,1,3,2,0:T(1,128)} %param.16) | copy-start | bytes 6916
  64.3 3.2 collective-permute-start.2
  66.3 4.7 %copy-start = (f32[6,3,4,8,128]{4,3,2,1,0:T(8,128)S(1)}, f32[6,3,4,8,128]{4,3,2,1,0:T(8,128)}, u32[]{:S(2)}) copy-start(f32[6,3,4,8,128]{4,3,2,1,0:T(8,128)} %param.12) | copy-start | bytes 884740
  67.6 3.4 collective-permute-start.3
  71.6 6.1 %collective-permute-start.4 = (f32[6,3,1,8,128]{4,0,3,2,1:T(8,128)S(1)}, f32[6,3,1,8,128]{4,0,3,2,1:T(8,128)S(1)}, u32[]{:S(2)}, u32[]{:S(2)}) collective-permute-start(f32[6,3,1,8,128]{4,0,3,2,1:T(8,128)S(1)} %fusion.43), channel_id=1, source_target_pairs={{16,0},{32,16},{48,32},{64,48},{80,64},{96,80},{112,96},{128,112},... | collective-permute-start | bytes 221192 | tf_op jit(solution)/shard_map/ppermute | solution.py:18
  77.8 7.3 %collective-permute-start.5 = (f32[6,3,5,1,128]{4,0,3,2,1:T(8,128)S(1)}, f32[6,3,5,1,128]{4,0,3,2,1:T(8,128)S(1)}, u32[]{:S(2)}, u32[]{:S(2)}) collective-permute-start(f32[6,3,5,1,128]{4,0,3,2,1:T(8,128)S(1)} %pad_maximum_fusion.4), channel_id=1, source_target_pairs={{1,0},{2,1},{3,2},{4,3},{5,4},{6,5},{7,6},{8,7},{9,8},{10,9},{11,1... | collective-permute-start | bytes 138248 | tf_op jit(solution)/shard_map/ppermute | solution.py:18
  132.4 3.2 collective-permute-start.6
  135.6 6.8 %collective-permute-start.7 = (f32[6,3,1,8,128]{4,0,3,2,1:T(8,128)S(1)}, f32[6,3,1,8,128]{4,0,3,2,1:T(8,128)S(1)}, u32[]{:S(2)}, u32[]{:S(2)}) collective-permute-start(f32[6,3,1,8,128]{4,0,3,2,1:T(8,128)S(1)} %pad_maximum_fusion.1), channel_id=1, source_target_pairs={{0,16},{16,32},{32,48},{48,64},{64,80},{80,96},{96,112},{112,128},... | collective-permute-start | bytes 221192 | tf_op jit(solution)/shard_map/ppermute | solution.py:18
  275.0 6.1 %collective-permute-start.8 = (f32[6,3,1,8,128]{4,0,3,2,1:T(8,128)S(1)}, f32[6,3,1,8,128]{4,0,3,2,1:T(8,128)S(1)}, u32[]{:S(2)}, u32[]{:S(2)}) collective-permute-start(f32[6,3,1,8,128]{4,0,3,2,1:T(8,128)S(1)} %slice.701), channel_id=1, source_target_pairs={{16,0},{32,16},{48,32},{64,48},{80,64},{96,80},{112,96},{128,112},... | collective-permute-start | bytes 221192 | tf_op jit(solution)/shard_map/ppermute | solution.py:18
  281.1 5.5 %collective-permute-start.9 = (f32[6,3,5,1,128]{4,0,3,2,1:T(8,128)S(1)}, f32[6,3,5,1,128]{4,0,3,2,1:T(8,128)S(1)}, u32[]{:S(2)}, u32[]{:S(2)}) collective-permute-start(f32[6,3,5,1,128]{4,0,3,2,1:T(8,128)S(1)} %pad_maximum_fusion.3), channel_id=1, source_target_pairs={{1,0},{2,1},{3,2},{4,3},{5,4},{6,5},{7,6},{8,7},{9,8},{10,9},{11,1... | collective-permute-start | bytes 138248 | tf_op jit(solution)/shard_map/ppermute | solution.py:18
  286.8 122.5 %copy-start.2 = (f32[4,8,128]{2,1,0:T(8,128)S(1)}, f32[4,8,128]{2,1,0:T(8,128)}, u32[]{:S(2)}) copy-start(f32[4,8,128]{2,1,0:T(8,128)} %param.14) | copy-start | bytes 49156
  295.4 2.6 collective-permute-start.10
  296.7 4.5 %collective-permute-start.11 = (f32[4,8,128]{2,1,0:T(8,128)S(1)}, f32[4,8,128]{2,1,0:T(8,128)S(1)}, u32[]{:S(2)}, u32[]{:S(2)}) collective-permute-start(f32[4,8,128]{2,1,0:T(8,128)S(1)} %mul.463), channel_id=1, source_target_pairs={{16,0},{32,16},{48,32},{64,48},{80,64},{96,80},{112,96},{128,112},... | collective-permute-start | bytes 49160 | tf_op jit(solution)/shard_map/ppermute | solution.py:31
  301.2 5.9 %collective-permute-start.12 = (f32[4,4,128]{2,1,0:T(4,128)S(1)}, f32[4,4,128]{2,1,0:T(4,128)S(1)}, u32[]{:S(2)}, u32[]{:S(2)}) collective-permute-start(f32[4,4,128]{2,1,0:T(4,128)S(1)} %get-tuple-element.272), channel_id=1, source_target_pairs={{0,1},{1,2},{2,3},{3,4},{4,5},{5,6},{6,7},{7,8},{8,9},{9,10},{10,1... | collective-permute-start | bytes 24584 | tf_op jit(solution)/shard_map/ppermute | solution.py:29
  304.4 5.0 %collective-permute-start.13 = (f32[4,4,128]{2,1,0:T(4,128)S(1)}, f32[4,4,128]{2,1,0:T(4,128)S(1)}, u32[]{:S(2)}, u32[]{:S(2)}) collective-permute-start(f32[4,4,128]{2,1,0:T(4,128)S(1)} %get-tuple-element.273), channel_id=1, source_target_pairs={{1,0},{2,1},{3,2},{4,3},{5,4},{6,5},{7,6},{8,7},{9,8},{10,9},{11,1... | collective-permute-start | bytes 24584 | tf_op jit(solution)/shard_map/ppermute | solution.py:31
